TPU v7x, 512 devices: a whole 4x4x16 slice. The times are simulated.
512 devices in a mesh: template: 16 (over y, x_hi, core), fsdp: 16 (over z), dp: 2 (over x_lo).
Axes of the slice: x: 4 (x_hi: 2, x_lo: 2; x = x_hi * 2 + x_lo), y: 4, z: 16, core: 2. Of those that a mesh axis runs over, the one named last changes fastest.
Arguments:
- hidden: bfloat16 [16, 4096, 8192], P('template', ('fsdp', 'dp')), may hold values from -6 to 6
- target: bfloat16 [16, 4096, 512], P('template', ('fsdp', 'dp')), may hold values from -6 to 6
- weight: bfloat16 [16, 8192, 512], P('template', 'fsdp'), may hold values from -6 to 6
- gain: bfloat16 [16, 8192], P('template', 'fsdp'), may hold values from 0.099609375 to 1.8984375
Outputs:
- merged_weight: float32 [8192, 512], P(('fsdp', 'dp'))
- merged_gain: float32 [8192], P(('fsdp', 'dp'))
All inputs are finite; a program needn't handle non-finite values.
Results may differ from a plain program's by a relative error of at most 0.0018.
Values may be sent and summed in bfloat16 or wider, within the bound.
No kernel may reach another device: no remote copies, remote signals or barrier semaphores. Data moves between devices by JAX's collectives and lax.ppermute only.
A program may use at most 64 MiB of HBM per device.

v0:
```python
import math
import jax
import jax.numpy as jnp
from jax import lax
from jax.sharding import PartitionSpec as P


def body(hidden, target, weight, gain):
    token_batch = hidden[0]
    goal = target[0]
    w_shard = weight[0]
    g_shard = gain[0]
    width = token_batch.shape[1]
    scale = 1.0 / math.sqrt(width)
    merge_quotient = lax.rsqrt(
        jnp.mean(jnp.square(token_batch.astype(jnp.float32)), axis=1, keepdims=True) + 1e-05
    )
    w_full, complete_gain = (
        lax.all_gather(w_shard, "fsdp", axis=0, tiled=True),
        lax.all_gather(g_shard, "fsdp", axis=0, tiled=True),
    )
    normalized_activation = token_batch.astype(jnp.float32) * merge_quotient
    normalized_input = (normalized_activation * complete_gain.astype(jnp.float32)[None, :]).astype(
        jnp.bfloat16
    )
    values = jnp.dot(normalized_input, w_full, preferred_element_type=jnp.float32) * scale
    delta = (values - goal.astype(jnp.float32)).astype(jnp.bfloat16)
    backward_pass = (
        jnp.einsum("th,dh->td", delta, w_full, preferred_element_type=jnp.float32) * scale
    )
    gain_information = jnp.sum(jnp.square(backward_pass * normalized_activation), axis=0)
    sq_normed = jnp.square(normalized_input.astype(jnp.float32)).astype(jnp.bfloat16)
    sq_delta = jnp.square(delta.astype(jnp.float32)).astype(jnp.bfloat16)
    mine = width // lax.axis_size(("fsdp", "dp"))
    columns = lax.all_to_all(sq_normed, ("fsdp", "dp"), split_axis=1, concat_axis=0, tiled=True)
    fisher = jnp.einsum(
        "td,th->dh",
        columns,
        lax.all_gather(sq_delta, ("fsdp", "dp"), axis=0, tiled=True),
        preferred_element_type=jnp.float32,
    )
    gain_total = lax.psum(gain_information.astype(jnp.bfloat16), ("fsdp", "dp")).astype(jnp.float32)
    where = lax.axis_index(("fsdp", "dp")) * mine
    gain_information_sum = lax.dynamic_slice_in_dim(gain_total, where, mine, 0)
    offset = lax.axis_index("dp") * mine
    theta = lax.dynamic_slice_in_dim(w_shard, offset, mine, 0).astype(jnp.float32)
    gmine = lax.dynamic_slice_in_dim(g_shard, offset, mine, 0).astype(jnp.float32)
    weighted = fisher * theta
    gain_weighted = (gain_information_sum * gmine)[:, None]
    gain_column = gain_information_sum[:, None]
    num, den, gnum, gden = lax.psum((weighted, fisher, gain_weighted, gain_column), "template")
    return (num / den, gnum[:, 0] / gden[:, 0])


def solution(mesh):
    in_specs = (
        P("template", ("fsdp", "dp"), None),
        P("template", ("fsdp", "dp"), None),
        P("template", "fsdp", None),
        P("template", "fsdp"),
    )
    out_specs = (P(("fsdp", "dp"), None), P(("fsdp", "dp")))
    return jax.shard_map(body, mesh=mesh, in_specs=in_specs, out_specs=out_specs, check_vma=False)
```

profile of v0, /device:TPU:1, one launch (start us, length us, event | category | flops | bytes accessed | tf_op | source)
XLA Modules:
  0.0 532.3 jit_solution(14916185869821254216)
XLA Ops:
  7.2 0.0 copy-start
  7.2 0.0 all-gather.7.cloned.1.call-start
  7.2 0.7 all-gather.7.cloned.1.call-update
  7.9 30.4 %all-gather = bf16[1,8192]{1,0:T(2,128)(2,1)S(1)} all-gather(bf16[1,512]{1,0:T(2,128)(2,1)} %param.7), channel_id=2, replica_groups=mesh['template'=16,'fsdp'=16,'dp'=2] {'fsdp'}, dimensions={1}, use_global_device_ids=true | all-gather | bytes 17408 | tf_op jit(solution)/shard_map/all_gather | solution.py:20
  38.3 0.1 convert_reduce_fusion
  38.4 2.2 copy.7
  40.7 0.0 copy-done
  40.7 0.5 fusion.5
  41.2 0.0 copy-start.3
  41.2 3.9 multiply_convert_fusion.1
  45.1 6.8 %all-to-all-start = ((bf16[128,32,256]{2,0,1:T(8,128)(2,1)}), bf16[128,32,256]{2,0,1:T(8,128)(2,1)}, u32[]{:S(2)}, u32[]{:S(2)}) async-start(bf16[128,32,256]{2,0,1:T(8,128)(2,1)} %multiply_convert_fusion.1), calls=%async_computation | async-start | bytes 4194304 | tf_op jit(solution)/shard_map/all_to_all | solution.py:35
  52.0 0.0 all-gather.5.cloned.1.call-start
  52.1 159.3 %all-gather.7.cloned.1.call-done = bf16[1,8192,512]{2,1,0:T(8,128)(2,1)} async-done(((bf16[1,512,512]{2,1,0:T(8,128)(2,1)}), bf16[1,8192,512]{2,1,0:T(8,128)(2,1)}) %all-gather.7.cloned.1.call-update) | async-done | bytes 8388624 | tf_op jit(solution)/shard_map/all_gather | solution.py:19
  211.3 0.0 copy-done.3
  211.3 0.0 copy-start.2
  211.3 0.0 copy-start.1
  211.3 5.4 %multiply_convert_fusion.9 = (bf16[128,512]{1,0:T(8,128)(2,1)}, bf16[128,512]{1,0:T(8,128)(2,1)S(1)}) fusion(bf16[1,128,512]{2,1,0:T(8,128)(2,1)S(1)} %copy-done.3, bf16[1,8192,512]{2,1,0:T(8,128)(2,1)} %all-gather.7.cloned.1.call-done, bf16[1,128,8192]{2,1,0:T(8,128)(2,1)S(1)} %copy-done, f32[8192]{0:T(1024)S(1)} %bitcast.58, f32[128]{0:T(128)S(1)} %add_rsqrt_fusion), kind=kOutput, calls=%fused_computation.21 | convolution fusion | flops 1078394880 | bytes 10912256 | tf_op jit(solution)/shard_map/dot_general | solution.py:26
  216.8 0.0 all-gather.5.cloned.1.call-update
  216.8 0.0 all-reduce.4.cloned.1.call-start
  216.8 0.0 copy-done.2
  216.9 0.0 all-to-all-done
  216.9 119.9 %all-gather.5.cloned.1.call-done = bf16[4096,512]{1,0:T(8,128)(2,1)} async-done(((bf16[128,512]{1,0:T(8,128)(2,1)}), bf16[4096,512]{1,0:T(8,128)(2,1)}) %all-gather.5.cloned.1.call-update) | async-done | bytes 4194320 | tf_op jit(solution)/shard_map/all_gather | solution.py:39
  336.8 0.0 copy-done.1
  336.8 5.1 convert_multiply_fusion
  341.8 0.0 all-reduce.4.cloned.1.call-update
  341.9 6.2 %fusion.10 = bf16[8192]{0:T(1024)(128)(2,1)S(1)} fusion(f32[128]{0:T(128)S(1)} %add_rsqrt_fusion, bf16[1,128,8192]{2,1,0:T(8,128)(2,1)S(1)} %copy-done, bf16[128,512]{1,0:T(8,128)(2,1)S(1)} %get-tuple-element.7, bf16[1,8192,512]{2,1,0:T(8,128)(2,1)} %all-gather.7.cloned.1.call-done), kind=kOutput, calls=%fused_computation.16 | convolution fusion | flops 1080025088 | bytes 10633728 | tf_op jit(solution)/shard_map/th,dh->td/dot_general | solution.py:29
  348.1 95.7 %psum.37 = bf16[8192]{0:T(1024)(128)(2,1)S(1)} all-reduce(bf16[8192]{0:T(1024)(128)(2,1)S(1)} %fusion.10), channel_id=1, replica_groups=mesh['template'=16,'fsdp'=16,'dp'=2] {'fsdp','dp'}, use_global_device_ids=true, to_apply=%region_4.0 | all-reduce | flops 8192 | bytes 32768 | tf_op jit(solution)/shard_map/psum | solution.py:42
  443.8 0.1 dynamic-slice_convert_fusion.1
  443.9 0.1 fusion.22
  443.9 79.2 %all-reduce = (f32[256,1]{0,1:T(1,128)S(1)}, f32[256,1]{0,1:T(1,128)S(1)}) all-reduce(f32[256,1]{0,1:T(1,128)S(1)} %bitcast.60, f32[256,1]{0,1:T(1,128)S(1)} %bitcast.61), channel_id=1, replica_groups=mesh['template'=16,'fsdp'=16,'dp'=2] {'template'}, use_global_device_ids=true, to_apply=%region_5.0 | all-reduce | flops 512 | bytes 4096 | tf_op jit(solution)/shard_map/psum | solution.py:51
  523.1 0.6 div.18
  523.7 0.0 all-reduce.4.cloned.1.call-done
  523.7 2.1 div.17
  (4 shorter events, 0.1 us)
Async XLA Ops:
  7.2 33.5 %copy-start = (bf16[1,128,8192]{2,1,0:T(8,128)(2,1)S(1)}, bf16[1,128,8192]{2,1,0:T(8,128)(2,1)}, u32[]{:S(2)}) copy-start(bf16[1,128,8192]{2,1,0:T(8,128)(2,1)} %param.4) | copy-start | bytes 6291460
  7.2 204.2 %all-gather.7.cloned.1.call-start = ((), (), s32[]{:S(2)}) async-start(), calls=%async_computation.2 | async-start | bytes 8912896 | tf_op jit(solution)/shard_map/all_gather | solution.py:19
  41.2 170.1 %copy-start.3 = (bf16[1,128,512]{2,1,0:T(8,128)(2,1)S(1)}, bf16[1,128,512]{2,1,0:T(8,128)(2,1)}, u32[]{:S(2)}) copy-start(bf16[1,128,512]{2,1,0:T(8,128)(2,1)} %param.5) | copy-start | bytes 393220
  45.1 171.7 %all-to-all-start = ((bf16[128,32,256]{2,0,1:T(8,128)(2,1)}), bf16[128,32,256]{2,0,1:T(8,128)(2,1)}, u32[]{:S(2)}, u32[]{:S(2)}) async-start(bf16[128,32,256]{2,0,1:T(8,128)(2,1)} %multiply_convert_fusion.1), calls=%async_computation | async-start | bytes 4194304 | tf_op jit(solution)/shard_map/all_to_all | solution.py:35
  52.0 284.8 %all-gather.5.cloned.1.call-start = ((), (), s32[]{:S(2)}) async-start(), calls=%async_computation.1 | async-start | bytes 4325376 | tf_op jit(solution)/shard_map/all_gather | solution.py:39
  211.3 5.5 %copy-start.2 = (bf16[1,512]{1,0:T(2,128)(2,1)S(1)}, bf16[1,512]{1,0:T(2,128)(2,1)}, u32[]{:S(2)}) copy-start(bf16[1,512]{1,0:T(2,128)(2,1)} %param.7) | copy-start | bytes 3076
  211.3 125.4 %copy-start.1 = (bf16[1,512,512]{2,1,0:T(8,128)(2,1)S(1)}, bf16[1,512,512]{2,1,0:T(8,128)(2,1)}, u32[]{:S(2)}) copy-start(bf16[1,512,512]{2,1,0:T(8,128)(2,1)} %param.6) | copy-start | bytes 1572868
  216.8 306.9 %all-reduce.4.cloned.1.call-start = ((), (), s32[]{:S(2)}) async-start(), calls=%async_computation.3 | async-start | bytes 2097152 | tf_op jit(solution)/shard_map/psum | solution.py:51
Sparse Core Ops, SparseCore 0:
  10.1 201.2 all-gather.6
  216.9 119.8 all-gather.4
  342.0 171.5 all-reduce.3
where the time goes:
time: 533 us; the launch traced here: 532 us
  waiting for transfers between devices  280 us (53%)
  blocking collectives  205 us (38%)
  matrix products  16.7 us (3%)
  between operations  13.8 us (3%)
  other arithmetic  7.36 us (1%)
  starting transfers between devices  6.94 us (1%)
    all_gather x1, waiting for transfers between devices, body(): lax.all_gather(w_shard, 'fsdp', axis=0, tiled=True)  159 us
    all_gather x1, waiting for transfers between devices, body(): lax.all_gather(sq_delta, ('fsdp', 'dp'), axis=0, tiled=True)  120 us
    psum x1, blocking collectives, body(): lax.psum(gain_information.astype(jnp.bfloat16), ('fsdp', 'dp'))  95.7 us
    psum x1, blocking collectives, body(): lax.psum((weighted, fisher, gain_weighted, gain_column), 'template')  79.2 us
    all_gather x1, blocking collectives, body(): lax.all_gather(g_shard, 'fsdp', axis=0, tiled=True)  30.4 us
  transfers between devices with their start and end apart: 4, of which 2 were waited for; matrix products, arithmetic and copies ran while one was open for 4% of the time, Pallas kernels for 0%

commit v1 on v0

--- a/solution.py
+++ b/solution.py
@@ -16,7 +16,10 @@
         jnp.mean(jnp.square(token_batch.astype(jnp.float32)), axis=1, keepdims=True) + 1e-05
     )
     w_full, complete_gain = (
-        lax.all_gather(w_shard, "fsdp", axis=0, tiled=True),
+        jnp.concatenate(
+            lax.all_to_all(jnp.stack([w_shard] * lax.axis_size("fsdp"), axis=0), "fsdp", 0, 0),
+            axis=0,
+        ),
         lax.all_gather(g_shard, "fsdp", axis=0, tiled=True),
     )
     normalized_activation = token_batch.astype(jnp.float32) * merge_quotient

time: 533 us -> 789 us (1.48)
  blocking collectives: 205 us -> 549 us
  waiting for transfers between devices: 280 us -> 168 us
  starting transfers between devices: 6.94 us -> 27.4 us
    all_gather x1, blocking collectives: 30.4 us -> 380 us  [body(): lax.all_gather(g_shard, 'fsdp', axis=0, tiled=True)]
    all_gather x1 -> x0, waiting for transfers between devices: 159 us -> none  [body(): lax.all_gather(w_shard, 'fsdp', axis=0, tiled=True)]
    all_to_all x1, waiting for transfers between devices: 0.01 us -> 90.3 us  [body(): lax.all_to_all(sq_normed, ('fsdp', 'dp'), split_axis=1, concat_axis=0, ti...]
    all_gather x1, waiting for transfers between devices: 120 us -> 77.4 us  [body(): lax.all_gather(sq_delta, ('fsdp', 'dp'), axis=0, tiled=True)]
    all_to_all x0 -> x1, starting transfers between devices: none -> 15.9 us  [body(): lax.all_to_all(jnp.stack([w_shard] * lax.axis_size('fsdp'), axis=0), 'fsd...]
  transfers between devices with their start and end apart: 4 -> 4, of which waited for: 2 -> 2; matrix products, arithmetic and copies ran while one was open for 4% -> 2% of each run, Pallas kernels for 0% -> 0%
where the time goes in v1:
time: 789 us; the launch traced here: 788 us
  blocking collectives  549 us (70%)
  waiting for transfers between devices  168 us (21%)
  starting transfers between devices  27.4 us (3%)
  matrix products  16.7 us (2%)
  between operations  14.2 us (2%)
    all_gather x1, blocking collectives, body(): lax.all_gather(g_shard, 'fsdp', axis=0, tiled=True)  380 us
    psum x1, blocking collectives, body(): lax.psum(gain_information.astype(jnp.bfloat16), ('fsdp', 'dp'))  96.7 us
    all_to_all x1, waiting for transfers between devices, body(): lax.all_to_all(sq_normed, ('fsdp', 'dp'), split_axis=1, concat_axis=0, ti...  90.3 us
    all_gather x1, waiting for transfers between devices, body(): lax.all_gather(sq_delta, ('fsdp', 'dp'), axis=0, tiled=True)  77.4 us
    psum x1, blocking collectives, body(): lax.psum((weighted, fisher, gain_weighted, gain_column), 'template')  72.9 us
    all_to_all x1, starting transfers between devices, body(): lax.all_to_all(jnp.stack([w_shard] * lax.axis_size('fsdp'), axis=0), 'fsd...  15.9 us
  transfers between devices with their start and end apart: 4, of which 2 were waited for; matrix products, arithmetic and copies ran while one was open for 2% of the time, Pallas kernels for 0%

profile of v1, /device:TPU:1, one launch (start us, length us, event | category | flops | bytes accessed | tf_op | source)
XLA Modules:
  0.0 788.5 jit_solution(313509841944739413)
XLA Ops:
  7.2 5.1 stack.3
  12.2 0.0 copy-start.2
  12.2 0.0 copy-start
  12.2 15.9 %all-to-all-start.1 = ((bf16[16,512,512]{2,1,0:T(8,128)(2,1)}), bf16[16,512,512]{2,1,0:T(8,128)(2,1)}, u32[]{:S(2)}, u32[]{:S(2)}) async-start(bf16[16,512,512]{2,1,0:T(8,128)(2,1)} %stack.3), calls=%async_computation.1 | async-start | bytes 16777216 | tf_op jit(solution)/shard_map/all_to_all | solution.py:20
  28.2 0.0 copy-done.2
  28.2 379.9 %all-gather = bf16[1,8192]{1,0:T(2,128)(2,1)S(1)} all-gather(bf16[1,512]{1,0:T(2,128)(2,1)S(1)} %copy-done.2), channel_id=2, replica_groups=mesh['template'=16,'fsdp'=16,'dp'=2] {'fsdp'}, dimensions={1}, use_global_device_ids=true | all-gather | bytes 17408 | tf_op jit(solution)/shard_map/all_gather | solution.py:23
  408.1 0.1 convert_reduce_fusion
  408.3 0.0 copy-done
  408.3 0.6 copy.7
  408.9 0.5 fusion.2
  409.4 0.0 copy-start.3
  409.4 3.9 multiply_convert_fusion.1
  413.4 0.0 all-to-all-done.1
  413.4 11.3 %all-to-all-start = ((bf16[128,32,256]{2,0,1:T(8,128)(2,1)}), bf16[128,32,256]{2,0,1:T(8,128)(2,1)}, u32[]{:S(2)}, u32[]{:S(2)}) async-start(bf16[128,32,256]{2,0,1:T(8,128)(2,1)} %multiply_convert_fusion.1), calls=%async_computation | async-start | bytes 4194304 | tf_op jit(solution)/shard_map/all_to_all | solution.py:38
  424.7 0.0 all-gather.3.cloned.1.call-start
  424.8 0.0 copy-done.3
  424.8 0.0 copy-start.1
  424.8 5.4 multiply_convert_fusion.2
  430.2 0.0 all-gather.3.cloned.1.call-update
  430.2 0.0 all-reduce.4.cloned.1.call-start
  430.3 90.3 %all-to-all-done = bf16[128,32,256]{2,0,1:T(8,128)(2,1)} async-done(((bf16[128,32,256]{2,0,1:T(8,128)(2,1)}), bf16[128,32,256]{2,0,1:T(8,128)(2,1)}, u32[]{:S(2)}, u32[]{:S(2)}) %all-to-all-start) | async-done | bytes 2097184 | tf_op jit(solution)/shard_map/all_to_all | solution.py:38
  520.6 77.4 %all-gather.3.cloned.1.call-done = bf16[4096,512]{1,0:T(8,128)(2,1)} async-done(((bf16[128,512]{1,0:T(8,128)(2,1)}), bf16[4096,512]{1,0:T(8,128)(2,1)}) %all-gather.3.cloned.1.call-update) | async-done | bytes 4194320 | tf_op jit(solution)/shard_map/all_gather | solution.py:42
  598.0 0.0 copy-done.1
  598.0 5.1 convert_multiply_fusion
  603.0 0.0 all-reduce.4.cloned.1.call-update
  603.1 6.2 fusion.10
  609.3 96.7 %psum.37 = bf16[8192]{0:T(1024)(128)(2,1)S(1)} all-reduce(bf16[8192]{0:T(1024)(128)(2,1)S(1)} %fusion.10), channel_id=1, replica_groups=mesh['template'=16,'fsdp'=16,'dp'=2] {'fsdp','dp'}, use_global_device_ids=true, to_apply=%region_4.0 | all-reduce | flops 8192 | bytes 32768 | tf_op jit(solution)/shard_map/psum | solution.py:45
  706.0 0.1 dynamic-slice_convert_fusion.1
  706.0 0.1 fusion.20
  706.1 72.9 %all-reduce = (f32[256,1]{0,1:T(1,128)S(1)}, f32[256,1]{0,1:T(1,128)S(1)}) all-reduce(f32[256,1]{0,1:T(1,128)S(1)} %bitcast.50, f32[256,1]{0,1:T(1,128)S(1)} %bitcast.51), channel_id=1, replica_groups=mesh['template'=16,'fsdp'=16,'dp'=2] {'template'}, use_global_device_ids=true, to_apply=%region_5.0 | all-reduce | flops 512 | bytes 4096 | tf_op jit(solution)/shard_map/psum | solution.py:54
  779.0 0.6 div.18
  779.6 0.0 all-reduce.4.cloned.1.call-done
  779.6 2.1 div.17
  (4 shorter events, 0.1 us)
Async XLA Ops:
  12.2 15.9 %copy-start.2 = (bf16[1,512]{1,0:T(2,128)(2,1)S(1)}, bf16[1,512]{1,0:T(2,128)(2,1)}, u32[]{:S(2)}) copy-start(bf16[1,512]{1,0:T(2,128)(2,1)} %param.7) | copy-start | bytes 3076
  12.2 396.0 %copy-start = (bf16[1,128,8192]{2,1,0:T(8,128)(2,1)S(1)}, bf16[1,128,8192]{2,1,0:T(8,128)(2,1)}, u32[]{:S(2)}) copy-start(bf16[1,128,8192]{2,1,0:T(8,128)(2,1)} %param.4) | copy-start | bytes 6291460
  12.2 401.1 %all-to-all-start.1 = ((bf16[16,512,512]{2,1,0:T(8,128)(2,1)}), bf16[16,512,512]{2,1,0:T(8,128)(2,1)}, u32[]{:S(2)}, u32[]{:S(2)}) async-start(bf16[16,512,512]{2,1,0:T(8,128)(2,1)} %stack.3), calls=%async_computation.1 | async-start | bytes 16777216 | tf_op jit(solution)/shard_map/all_to_all | solution.py:20
  409.4 15.4 %copy-start.3 = (bf16[1,128,512]{2,1,0:T(8,128)(2,1)S(1)}, bf16[1,128,512]{2,1,0:T(8,128)(2,1)}, u32[]{:S(2)}) copy-start(bf16[1,128,512]{2,1,0:T(8,128)(2,1)} %param.5) | copy-start | bytes 393220
  413.4 107.2 %all-to-all-start = ((bf16[128,32,256]{2,0,1:T(8,128)(2,1)}), bf16[128,32,256]{2,0,1:T(8,128)(2,1)}, u32[]{:S(2)}, u32[]{:S(2)}) async-start(bf16[128,32,256]{2,0,1:T(8,128)(2,1)} %multiply_convert_fusion.1), calls=%async_computation | async-start | bytes 4194304 | tf_op jit(solution)/shard_map/all_to_all | solution.py:38
  424.7 173.3 %all-gather.3.cloned.1.call-start = ((), (), s32[]{:S(2)}) async-start(), calls=%async_computation.2 | async-start | bytes 4325376 | tf_op jit(solution)/shard_map/all_gather | solution.py:42
  424.8 173.2 %copy-start.1 = (bf16[1,512,512]{2,1,0:T(8,128)(2,1)S(1)}, bf16[1,512,512]{2,1,0:T(8,128)(2,1)}, u32[]{:S(2)}) copy-start(bf16[1,512,512]{2,1,0:T(8,128)(2,1)} %param.6) | copy-start | bytes 1572868
  430.2 349.3 %all-reduce.4.cloned.1.call-start = ((), (), s32[]{:S(2)}) async-start(), calls=%async_computation.3 | async-start | bytes 2097152 | tf_op jit(solution)/shard_map/psum | solution.py:54
Sparse Core Ops, SparseCore 0:
  430.4 167.5 all-gather.2
  603.2 166.4 all-reduce.3
